TPU v7x, 512 devices: a whole 4x4x16 slice. The times are simulated.
512 devices in a mesh: dp: 64 (over z, x_hi, core), fsdp: 8 (over x_lo, y).
Axes of the slice: x: 4 (x_hi: 2, x_lo: 2; x = x_hi * 2 + x_lo), y: 4, z: 16, core: 2. Of those that a mesh axis runs over, the one named last changes fastest.
Arguments:
- states: bfloat16 [128, 512, 5120], P('dp', None, 'fsdp'), may hold values from -240 to 240
- valid_counts: int32 [128], P('dp'), may hold values from 32 to 512
- section_ids: int32 [128], replicated, may hold values from 0 to 63, never falling along the last dimension, each value on 1 to 6 neighbouring positions
- norm_gain: bfloat16 [5120], P('fsdp'), may hold values from 0.099609375 to 1.8984375
- head_weight: bfloat16 [5120, 2048], P('fsdp'), may hold values from -0.078125 to 0.078125
Outputs:
- embeddings: float32 [64, 3840], P('dp')
Inputs may be any that keep to these rules, and one draw needn't show every extreme that they name: `section_ids`: section numbers never fall along the spans; every one of the 64 sections has 1 to 6 spans.
All inputs are finite; a program needn't handle non-finite values.
Results may differ from a plain program's by a relative error of at most 0.0003.
Values sent between devices are 32-bit elements; how exact they have to be, the bound alone decides.
No kernel may reach another device: no remote copies, remote signals or barrier semaphores. Data moves between devices by JAX's collectives and lax.ppermute only.
A program may use at most 64 MiB of HBM per device.

v0:
```python
import jax
import jax.numpy as jnp
from jax import lax
from jax.sharding import PartitionSpec as P

D = 5120
epsilon = 1e-06


def nested(projected):
    width = projected.shape[1]
    pieces = []
    for level in (width // 8, width // 4, width // 2, width):
        front = projected[:, :level]
        pieces.append(front * lax.rsqrt(jnp.mean(front * front, axis=1, keepdims=True) + epsilon))
    return jnp.concatenate(pieces, axis=1)


def local(states, valid_counts, section_ids, norm_gain, head_weight):
    values = states.astype(jnp.float32)
    partial_squares = jnp.sum(values * values, axis=-1)
    squares = lax.psum(partial_squares, "fsdp")
    scale = lax.rsqrt(squares / D + epsilon)
    slots = jnp.arange(states.shape[1], dtype=jnp.int32)
    used = (slots[None, :] < valid_counts[:, None]).astype(jnp.float32)
    weights = scale * used
    sums = jnp.einsum("cl,cld->cd", weights, values, precision=lax.Precision.HIGHEST)
    pooled = (
        sums / valid_counts.astype(jnp.float32)[:, None] * norm_gain.astype(jnp.float32)[None, :]
    )
    groups = lax.axis_size("dp")
    local_spans = pooled.shape[0]
    sec_local = local_spans // 2
    total_sections = sec_local * groups
    me = lax.axis_index("dp")
    my_ids = lax.dynamic_slice_in_dim(section_ids, me * local_spans, local_spans, 0)
    labels = jnp.arange(total_sections, dtype=jnp.int32)
    contrib = jnp.zeros((total_sections, pooled.shape[1]), jnp.float32)
    for c in range(local_spans):
        contrib = contrib + jnp.where((labels == my_ids[c])[:, None], pooled[c][None, :], 0.0)
    received = lax.all_to_all(contrib, "dp", 0, 0, tiled=True)
    section_sums = jnp.sum(received.reshape(groups, sec_local, -1), axis=0)
    terms = jnp.dot(section_sums, head_weight.astype(jnp.float32), precision=lax.Precision.HIGHEST)
    projected = lax.psum(terms, "fsdp")
    return nested(projected)


def solution(mesh):
    in_specs = (P("dp", None, "fsdp"), P("dp"), P(), P("fsdp"), P("fsdp", None))
    out_specs = P("dp", None)
    return jax.shard_map(local, mesh=mesh, in_specs=in_specs, out_specs=out_specs, check_vma=False)
```

profile of v0, /device:TPU:8, one launch (start us, length us, event | category | flops | bytes accessed | tf_op | source)
XLA Modules:
  0.0 90.2 jit_solution(11067146023472021934)
XLA Ops:
  0.0 0.0 copy-start
  0.0 0.8 convert_element_type.12
  0.8 0.7 dynamic_slice.3
  1.5 0.6 fusion.5
  2.1 0.7 convert_element_type.13
  2.8 1.6 %multiply_reduce_fusion = f32[2,512]{1,0:T(2,128)S(1)} fusion(bf16[2,512,640]{2,1,0:T(8,128)(2,1)} %param.5), kind=kLoop, calls=%fused_computation | loop fusion | flops 1965056 | bytes 1314816 | tf_op jit(solution)/shard_map/reduce_sum | solution.py:21
  4.5 21.8 %psum.14 = f32[2,512]{1,0:T(2,128)S(1)} all-reduce(f32[2,512]{1,0:T(2,128)S(1)} %multiply_reduce_fusion), channel_id=1, replica_groups=mesh['dp'=64,'fsdp'=8] {'fsdp'}, use_global_device_ids=true, to_apply=%region_1.0 | all-reduce | flops 1024 | bytes 8192 | tf_op jit(solution)/shard_map/psum | solution.py:22
  26.2 0.7 fusion.2
  27.0 1.9 %fusion.3 = f32[2,1,640]{2,1,0:T(1,128)S(1)} fusion(bf16[2,512,640]{2,1,0:T(8,128)(2,1)} %param.5, f32[2,512,1]{1,0,2:T(2,128)S(1)} %fusion.2), kind=kOutput, calls=%fused_computation.10 | convolution fusion | flops 7864320 | bytes 1319936 | tf_op jit(solution)/shard_map/cl,cld->cd/dot_general | solution.py:27
  28.9 0.1 fusion.1
  29.0 1.3 %iota_compare_fusion = (pred[64]{0:T(512)(128)(4,1)S(1)}, pred[64]{0:T(512)(128)(4,1)S(1)}) fusion(s32[]{:T(128)} %bitcast.3, s32[]{:T(128)} %bitcast), kind=kLoop, calls=%fused_computation.21 | loop fusion | flops 128 | bytes 136 | tf_op jit(solution)/shard_map/eq | solution.py:40
  30.3 0.2 fusion
  30.6 32.8 %all_to_all.6 = f32[64,1,640]{2,1,0:T(1,128)S(1)} all-to-all(f32[64,1,640]{2,1,0:T(1,128)S(1)} %fusion), channel_id=1, replica_groups=mesh['dp'=64,'fsdp'=8] {'dp'}, dimensions={0} | all-to-all | bytes 327680 | tf_op jit(solution)/shard_map/all_to_all | solution.py:41
  63.4 0.1 reduce_sum.55
  63.6 0.0 copy-done
  63.6 1.1 %fusion.6 = f32[1,2048]{1,0:T(1,128)S(1)} fusion(f32[640,1]{0,1:T(1,128)S(1)} %reshape.153, bf16[640,2048]{1,0:T(8,128)(2,1)S(1)} %copy-done), kind=kOutput, calls=%fused_computation.24 | convolution fusion | flops 15728640 | bytes 2632192 | tf_op jit(solution)/shard_map/dot_general | solution.py:43
  64.7 19.6 %psum.15 = f32[1,2048]{1,0:T(1,128)S(1)} all-reduce(f32[1,2048]{1,0:T(1,128)S(1)} %fusion.6), channel_id=1, replica_groups=mesh['dp'=64,'fsdp'=8] {'fsdp'}, use_global_device_ids=true, to_apply=%region_3.4 | all-reduce | flops 2048 | bytes 16384 | tf_op jit(solution)/shard_map/psum | solution.py:44
  84.3 0.6 multiply_reduce_fusion.1
  84.9 0.7 multiply_reduce_fusion.2
  85.6 0.6 multiply_reduce_fusion.3
  86.2 0.6 multiply_reduce_fusion.4
  89.5 0.6 pad_maximum_fusion
  (6 shorter events, 0.1 us)
Async XLA Ops:
  0.0 63.6 %copy-start = (bf16[640,2048]{1,0:T(8,128)(2,1)S(1)}, bf16[640,2048]{1,0:T(8,128)(2,1)}, u32[]{:S(2)}) copy-start(bf16[640,2048]{1,0:T(8,128)(2,1)} %param.9) | copy-start | bytes 7864324
where the time goes:
time: 90.5 us; the launch traced here: 90.2 us
  blocking collectives  74.2 us (82%)
  other arithmetic  8.81 us (10%)
  matrix products  3.06 us (3%)
  between operations  2.77 us (3%)
  local copies, waits for them, and re-layouts  1.36 us (2%)
    all_to_all x1, blocking collectives, local(): received = lax.all_to_all(contrib, 'dp', 0, 0, tiled=True)  32.8 us
    psum x1, blocking collectives, local(): squares = lax.psum(partial_squares, 'fsdp')  21.8 us
    psum x1, blocking collectives, local(): projected = lax.psum(terms, 'fsdp')  19.6 us
    reduce_sum x4, other arithmetic, nested(): jnp.mean(front * front, axis=1, keepdims=True) + epsilon  2.53 us
    dot_general x1, matrix products, local(): jnp.einsum('cl,cld->cd', weights, values, precision=lax.Precision.HIGHEST)  1.94 us

commit v1 on v0

--- a/solution.py
+++ b/solution.py
@@ -19,7 +19,7 @@
 def local(states, valid_counts, section_ids, norm_gain, head_weight):
     values = states.astype(jnp.float32)
     partial_squares = jnp.sum(values * values, axis=-1)
-    squares = lax.psum(partial_squares, "fsdp")
+    squares = jnp.sum(lax.all_gather(partial_squares, "fsdp"), axis=0)
     scale = lax.rsqrt(squares / D + epsilon)
     slots = jnp.arange(states.shape[1], dtype=jnp.int32)
     used = (slots[None, :] < valid_counts[:, None]).astype(jnp.float32)

time: 90.5 us -> 102 us (1.13)
  the two profiles are of different devices: /device:TPU:8 before, /device:TPU:2 now
where the time goes in v1:
time: 102 us; the launch traced here: 101 us
  blocking collectives  85.2 us (84%)
  other arithmetic  8.83 us (9%)
  matrix products  3.06 us (3%)
  between operations  2.77 us (3%)
  local copies, waits for them, and re-layouts  1.36 us (1%)
    all_to_all x1, blocking collectives, local(): received = lax.all_to_all(contrib, 'dp', 0, 0, tiled=True)  35.3 us
    all_gather x1, blocking collectives, local(): squares = jnp.sum(lax.all_gather(partial_squares, 'fsdp'), axis=0)  29.8 us
    psum x1, blocking collectives, local(): projected = lax.psum(terms, 'fsdp')  20.1 us
    reduce_sum x4, other arithmetic, nested(): jnp.mean(front * front, axis=1, keepdims=True) + epsilon  2.53 us

profile of v1, /device:TPU:2, one launch (start us, length us, event | category | flops | bytes accessed | tf_op | source)
XLA Modules:
  0.0 101.2 jit_solution(11956574383922496008)
XLA Ops:
  0.0 0.0 copy-start
  0.0 0.8 convert_element_type.12
  0.8 0.7 dynamic_slice.3
  1.5 0.6 fusion.5
  2.1 0.7 convert_element_type.13
  2.8 1.6 %multiply_reduce_fusion = f32[2,512]{1,0:T(2,128)S(1)} fusion(bf16[2,512,640]{2,1,0:T(8,128)(2,1)} %param.5), kind=kLoop, calls=%fused_computation | loop fusion | flops 1965056 | bytes 1314816 | tf_op jit(solution)/shard_map/reduce_sum | solution.py:21
  4.5 29.8 %all-gather.1 = f32[8,2,512]{2,1,0:T(2,128)S(1)} all-gather(f32[1,2,512]{2,1,0:T(2,128)S(1)} %bitcast.13), channel_id=2, replica_groups=mesh['dp'=64,'fsdp'=8] {'fsdp'}, dimensions={0}, use_global_device_ids=true | all-gather | bytes 36864 | tf_op jit(solution)/shard_map/all_gather | solution.py:22
  34.3 0.7 fusion.2
  35.0 1.9 %fusion.3 = f32[2,1,640]{2,1,0:T(1,128)S(1)} fusion(bf16[2,512,640]{2,1,0:T(8,128)(2,1)} %param.5, f32[2,512,1]{1,0,2:T(2,128)S(1)} %fusion.2), kind=kOutput, calls=%fused_computation.10 | convolution fusion | flops 7864320 | bytes 1319936 | tf_op jit(solution)/shard_map/cl,cld->cd/dot_general | solution.py:27
  36.9 0.1 fusion.1
  37.1 1.3 %iota_compare_fusion = (pred[64]{0:T(512)(128)(4,1)S(1)}, pred[64]{0:T(512)(128)(4,1)S(1)}) fusion(s32[]{:T(128)} %bitcast.4, s32[]{:T(128)} %bitcast), kind=kLoop, calls=%fused_computation.21 | loop fusion | flops 128 | bytes 136 | tf_op jit(solution)/shard_map/eq | solution.py:40
  38.4 0.2 fusion
  38.6 35.3 %all_to_all.6 = f32[64,1,640]{2,1,0:T(1,128)S(1)} all-to-all(f32[64,1,640]{2,1,0:T(1,128)S(1)} %fusion), channel_id=1, replica_groups=mesh['dp'=64,'fsdp'=8] {'dp'}, dimensions={0} | all-to-all | bytes 327680 | tf_op jit(solution)/shard_map/all_to_all | solution.py:41
  74.0 0.1 reduce_sum.65
  74.1 0.0 copy-done
  74.1 1.1 %fusion.6 = f32[1,2048]{1,0:T(1,128)S(1)} fusion(f32[640,1]{0,1:T(1,128)S(1)} %reshape.157, bf16[640,2048]{1,0:T(8,128)(2,1)S(1)} %copy-done), kind=kOutput, calls=%fused_computation.24 | convolution fusion | flops 15728640 | bytes 2632192 | tf_op jit(solution)/shard_map/dot_general | solution.py:43
  75.2 20.1 %psum.7 = f32[1,2048]{1,0:T(1,128)S(1)} all-reduce(f32[1,2048]{1,0:T(1,128)S(1)} %fusion.6), channel_id=1, replica_groups=mesh['dp'=64,'fsdp'=8] {'fsdp'}, use_global_device_ids=true, to_apply=%region_3.4 | all-reduce | flops 2048 | bytes 16384 | tf_op jit(solution)/shard_map/psum | solution.py:44
  95.3 0.6 multiply_reduce_fusion.1
  95.9 0.7 multiply_reduce_fusion.2
  96.6 0.6 multiply_reduce_fusion.3
  97.2 0.6 multiply_reduce_fusion.4
  100.6 0.6 pad_maximum_fusion
  (7 shorter events, 0.1 us)
Async XLA Ops:
  0.0 74.1 %copy-start = (bf16[640,2048]{1,0:T(8,128)(2,1)S(1)}, bf16[640,2048]{1,0:T(8,128)(2,1)}, u32[]{:S(2)}) copy-start(bf16[640,2048]{1,0:T(8,128)(2,1)} %param.9) | copy-start | bytes 7864324
